TPU v7x, 128 devices: a whole 4x4x4 slice. The times are simulated.
128 devices in a mesh: cp: 16 (over z, x), grp: 8 (over y, core).
Axes of the slice: x: 4, y: 4, z: 4, core: 2. Of those that a mesh axis runs over, the one named last changes fastest.
Arguments:
- queries: bfloat16 [32768, 8192], P(('cp', 'grp')), may hold values from -60 to 60
- keys: bfloat16 [32768, 1024], P(('cp', 'grp')), may hold values from -4 to 4
- values: bfloat16 [32768, 1024], P(('cp', 'grp')), may hold values from -6 to 6
- doc_lengths: int32 [16, 3], P('cp'), may hold values from 1 to 1536, 2048 in all within a row
- send_tile: int32 [128, 32], P(('cp', 'grp')), may hold values from 0 to 16, as said below
- take_slot: int32 [128, 16], P(('cp', 'grp')), may hold values from 0 to 31, as said below
Outputs:
- attended: bfloat16 [32768, 8192], P(('cp', 'grp'))
Inputs may be any that keep to these rules, and one draw needn't show every extreme that they name: `send_tile`: entry c2 * 2 + s of row d = c * 8 + g names the arrival tile (0 to 15) that device (c, g) sends in slot s to device (c2, g), and 16 marks an empty slot. Every tile of a device is sent exactly once; each device sends 2 tiles to each of exactly 8 peers and none to the others. `take_slot`: row d2 lists, for each owner tile of device d2, the received slot c * 2 + s (slot s of the tiles sent by device (c, g) of the same g) that fills it; every filled send slot fills exactly one owner tile, so each device receives from exactly 8 peers.
All inputs are finite; a program needn't handle non-finite values.
Results may differ from a plain program's by a relative error of at most 0.0037.
Values may be sent and summed in bfloat16 or wider, within the bound.
No kernel may reach another device: no remote copies, remote signals or barrier semaphores. Data moves between devices by JAX's collectives and lax.ppermute only.
A program may use at most 128 MiB of HBM per device.

v0:
```python
import math

import jax
import jax.numpy as jnp
from jax import lax
from jax.sharding import PartitionSpec as P

QUERY_HEADS = 64
KEY_VALUE_HEADS = 8
HEAD_SIZE = 128


def local(queries, keys, values, doc_lengths, send_tile, take_slot):
    tok_rows = queries.shape[0]
    peer_count = lax.axis_size("cp")
    member_count = lax.axis_size("grp")
    tile_rows = tok_rows // peer_count
    slot_count = send_tile.shape[1] // peer_count
    chosen = send_tile[0]
    placed = take_slot[0]

    def outgoing(source):
        tiled = source.reshape(peer_count, tile_rows, source.shape[1])
        picked = jnp.take(tiled, chosen, axis=0, mode="fill", fill_value=0)
        return picked.reshape(peer_count * slot_count * tile_rows, source.shape[1])

    def incoming(source):
        tiled = source.reshape(peer_count * slot_count, tile_rows, source.shape[1])
        return jnp.take(tiled, placed, axis=0).reshape(tok_rows, source.shape[1])

    got_queries, got_keys, got_values = (
        lax.all_to_all(outgoing(queries), "cp", split_axis=0, concat_axis=0, tiled=True),
        lax.all_to_all(outgoing(keys), "cp", split_axis=0, concat_axis=0, tiled=True),
        lax.all_to_all(outgoing(values), "cp", split_axis=0, concat_axis=0, tiled=True),
    )
    own_queries = incoming(got_queries)
    all_keys, all_values = (
        lax.all_gather(incoming(got_keys), "grp", axis=0, tiled=True),
        lax.all_gather(incoming(got_values), "grp", axis=0, tiled=True),
    )
    member = lax.axis_index("grp")
    group_length = member_count * tok_rows
    doc_ends = jnp.cumsum(doc_lengths[0])
    positions = jnp.arange(group_length, dtype=jnp.int32)
    doc_all = jnp.sum((positions[:, None] >= doc_ends[None, :]).astype(jnp.int32), axis=1)
    query_pos = member * tok_rows + jnp.arange(tok_rows, dtype=jnp.int32)
    doc_query = lax.dynamic_slice_in_dim(doc_all, member * tok_rows, tok_rows)
    allowed = (doc_query[:, None] == doc_all[None, :]) & (positions[None, :] <= query_pos[:, None])
    queries_per_group = QUERY_HEADS // KEY_VALUE_HEADS
    head_width = queries_per_group * HEAD_SIZE
    score_scale = 1.0 / math.sqrt(HEAD_SIZE)

    def single_head_output(head_number_index, result):
        query_head = lax.dynamic_slice_in_dim(
            own_queries, head_number_index * head_width, head_width, 1
        )
        query_head = query_head.reshape(tok_rows, queries_per_group, HEAD_SIZE)
        key_head = lax.dynamic_slice_in_dim(all_keys, head_number_index * HEAD_SIZE, HEAD_SIZE, 1)
        value_head = lax.dynamic_slice_in_dim(
            all_values, head_number_index * HEAD_SIZE, HEAD_SIZE, 1
        )
        scores = (
            jnp.einsum("qgd,kd->gqk", query_head, key_head, preferred_element_type=jnp.float32)
            * score_scale
        )
        scores = jnp.where(allowed[None], scores, -jnp.inf)
        row_max = jnp.max(scores, axis=2, keepdims=True)
        weights = jnp.exp(scores - row_max)
        totals = jnp.sum(weights, axis=2)
        rounded = weights.astype(jnp.bfloat16)
        summed = jnp.einsum("gqk,kd->qgd", rounded, value_head, preferred_element_type=jnp.float32)
        mixed = (summed / jnp.transpose(totals)[:, :, None]).astype(jnp.bfloat16)
        return lax.dynamic_update_slice_in_dim(
            result, mixed.reshape(tok_rows, head_width), head_number_index * head_width, 1
        )

    starting_state = jnp.zeros((tok_rows, QUERY_HEADS * HEAD_SIZE), jnp.bfloat16)
    return lax.fori_loop(0, KEY_VALUE_HEADS, single_head_output, starting_state)


def solution(mesh):
    return jax.shard_map(
        local,
        mesh=mesh,
        in_specs=(
            P(("cp", "grp"), None),
            P(("cp", "grp"), None),
            P(("cp", "grp"), None),
            P("cp", None),
            P(("cp", "grp"), None),
            P(("cp", "grp"), None),
        ),
        out_specs=P(("cp", "grp"), None),
        check_vma=False,
    )
```

profile of v0, /device:TPU:16, one launch (start us, length us, event | category | flops | bytes accessed | tf_op | source)
XLA Modules:
  0.0 463.5 jit_solution(10618601127550349147)
XLA Ops:
  6.5 0.7 compare_and_fusion.2
  7.3 0.7 compare_select_fusion.2
  7.9 0.6 gather_fusion.4
  8.6 1.7 gather_fusion.2
  10.2 1.2 broadcast_select_fusion
  11.4 24.8 %all_to_all.24 = bf16[16,32,1024]{2,1,0:T(8,128)(2,1)S(1)} all-to-all(bf16[16,32,1024]{2,1,0:T(8,128)(2,1)S(1)} %bitcast.90), channel_id=1, replica_groups=mesh['cp'=16,'grp'=8] {'cp'}, dimensions={0} | all-to-all | bytes 2097152 | tf_op jit(solution)/shard_map/all_to_all | solution.py:34
  36.2 3.7 all-to-all-start.1
  40.0 0.6 gather_fusion.3
  40.6 15.6 %all-to-all-done.1 = bf16[16,32,1024]{2,1,0:T(8,128)(2,1)S(1)} async-done(((bf16[16,32,1024]{2,1,0:T(8,128)(2,1)}), bf16[16,32,1024]{2,1,0:T(8,128)(2,1)S(1)}, u32[]{:S(2)}, u32[]{:S(2)}) %all-to-all-start.1) | async-done | bytes 1048608 | tf_op jit(solution)/shard_map/all_to_all | solution.py:33
  56.2 0.6 gather_fusion.5
  56.8 1.2 broadcast_select_fusion.2
  58.5 0.7 reduce.3
  59.5 7.3 %gather_fusion = bf16[32,16,8192]{2,1,0:T(8,128)(2,1)} fusion(bf16[16,16,8192]{2,1,0:T(8,128)(2,1)} %bitcast.87, s32[1024]{0:T(1024)S(1)} %pad_clamp_fusion.1), kind=kCustom, calls=%fused_computation.4 | custom fusion | bytes 16777344 | tf_op jit(solution)/shard_map/jit(_take)/gather | solution.py:24
  66.7 7.2 %bitcast_select_fusion.1 = bf16[16,32,8192]{2,1,0:T(8,128)(2,1)} fusion(pred[16,32]{1,0:T(8,128)(4,1)S(1)} %copy.25, bf16[16,32,8192]{2,1,0:T(8,128)(2,1)} %bitcast.86), kind=kLoop, calls=%fused_computation.29 | loop fusion | flops 4194304 | bytes 16777728 | tf_op jit(solution)/shard_map/jit(_take)/select_n | solution.py:24
  73.9 4.9 %all-to-all-start.2 = ((bf16[16,32,8192]{2,1,0:T(8,128)(2,1)}), bf16[16,32,8192]{2,1,0:T(8,128)(2,1)}, u32[]{:S(2)}, u32[]{:S(2)}) async-start(bf16[16,32,8192]{2,1,0:T(8,128)(2,1)} %bitcast_select_fusion.1), calls=%async_computation.2 | async-start | bytes 16777216 | tf_op jit(solution)/shard_map/all_to_all | solution.py:32
  80.2 119.3 %all-to-all-done.2 = bf16[16,32,8192]{2,1,0:T(8,128)(2,1)} async-done(((bf16[16,32,8192]{2,1,0:T(8,128)(2,1)}), bf16[16,32,8192]{2,1,0:T(8,128)(2,1)}, u32[]{:S(2)}, u32[]{:S(2)}) %all-to-all-start.2) | async-done | bytes 8388640 | tf_op jit(solution)/shard_map/all_to_all | solution.py:32
  199.4 6.2 %gather_fusion.1 = bf16[16,16,8192]{2,1,0:T(8,128)(2,1)} fusion(bf16[32,16,8192]{2,1,0:T(8,128)(2,1)} %bitcast.15, s32[1024]{0:T(1024)S(1)} %pad_clamp_fusion), kind=kCustom, calls=%fused_computation.5 | custom fusion | bytes 8388672 | tf_op jit(solution)/shard_map/jit(_take)/gather | solution.py:29
  205.7 4.6 bitcast_select_fusion.2
  210.3 2.5 broadcast_in_dim.88.clone
  212.7 242.9 %while.14 = (s32[]{:T(128)}, bf16[256,8192]{1,0:T(8,128)(2,1)}, bf16[2048,1024]{1,0:T(8,128)(2,1)}, bf16[2048,1024]{1,0:T(8,128)(2,1)}, bf16[256,8192]{1,0:T(8,1...) while((s32[]{:T(128)}, bf16[256,8192]{1,0:T(8,128)(2,1)}, ...), condition=%wide.region_5.8_spmd.clone, body=%wide.region_2.0_spmd.clone.sunk | while | flops 2195714048 | bytes 58771696 | solution.py:78
  212.7 0.5 fusion.35
  213.3 1.1 constant_dynamic-slice_fusion.2
  214.6 8.2 %fusion.36 = (f32[8,256]{1,0:T(8,128)S(1)}, f32[2048,256,8]{1,0,2:T(8,128)}) fusion(pred[256,2048]{0,1:T(8,128)(4,1)S(1)} %fusion.35, bf16[256,8,128]{0,2,1:T(8,128)(2,1)S(1)} %bitcast.85, bf16[2048,1024]{1,0:T(8,128)(2,1)} %get-tuple-element.266, s32[]{:T(128)S(6)} %select_n.147), kind=kOutput, calls=%fused_computation.11.clone.1 | convolution fusion | flops 1086322688 | bytes 18358276 | tf_op jit(solution)/shard_map/while/body/eval_jaxpr/qgd,kd->gqk/dot_general | solution.py:63
  222.8 9.2 %fusion.37 = f32[8,256]{1,0:T(8,128)S(1)} fusion(f32[2048,256,8]{1,0,2:T(8,128)} %get-tuple-element.235, f32[8,256]{1,0:T(8,128)S(1)} %get-tuple-element.236, pred[256,2048]{0,1:T(8,128)(4,1)S(1)} %fusion.35), kind=kLoop, calls=%fused_computation.9.clone.1 | loop fusion | flops 16775168 | bytes 17317888 | tf_op jit(solution)/shard_map/while/body/eval_jaxpr/reduce_sum | solution.py:69
  231.9 10.1 %divide_convert_fusion.2 = bf16[256,8,128]{0,2,1:T(8,128)(2,1)S(1)} fusion(f32[2048,256,8]{1,0,2:T(8,128)} %get-tuple-element.235, f32[8,256]{1,0:T(8,128)S(1)} %get-tuple-element.236, pred[256,2048]{0,1:T(8,128)(4,1)S(1)} %fusion.35, f32[256,8]{0,1:T(8,128)S(1)} %bitcast.96, bf16[2048,1024]{1,0:T(8,128)(2,1)} %get-tuple-element.265, s32[]{:T(128)S(6)} %select_n.147), kind=kOutput, calls=%fused_computation.17.clone.1 | convolution fusion | flops 1091043328 | bytes 18366468 | tf_op jit(solution)/shard_map/while/body/eval_jaxpr/gqk,kd->qgd/dot_general | solution.py:71
  242.3 0.8 constant_dynamic-update-slice_fusion.2
  243.1 0.5 fusion.35
  243.6 1.1 constant_dynamic-slice_fusion.2
  244.9 8.2 %fusion.36 = (f32[8,256]{1,0:T(8,128)S(1)}, f32[2048,256,8]{1,0,2:T(8,128)}) fusion(pred[256,2048]{0,1:T(8,128)(4,1)S(1)} %fusion.35, bf16[256,8,128]{0,2,1:T(8,128)(2,1)S(1)} %bitcast.85, bf16[2048,1024]{1,0:T(8,128)(2,1)} %get-tuple-element.266, s32[]{:T(128)S(6)} %select_n.147), kind=kOutput, calls=%fused_computation.11.clone.1 | convolution fusion | flops 1086322688 | bytes 18358276 | tf_op jit(solution)/shard_map/while/body/eval_jaxpr/qgd,kd->gqk/dot_general | solution.py:63
  253.1 9.2 %fusion.37 = f32[8,256]{1,0:T(8,128)S(1)} fusion(f32[2048,256,8]{1,0,2:T(8,128)} %get-tuple-element.235, f32[8,256]{1,0:T(8,128)S(1)} %get-tuple-element.236, pred[256,2048]{0,1:T(8,128)(4,1)S(1)} %fusion.35), kind=kLoop, calls=%fused_computation.9.clone.1 | loop fusion | flops 16775168 | bytes 17317888 | tf_op jit(solution)/shard_map/while/body/eval_jaxpr/reduce_sum | solution.py:69
  262.3 10.1 %divide_convert_fusion.2 = bf16[256,8,128]{0,2,1:T(8,128)(2,1)S(1)} fusion(f32[2048,256,8]{1,0,2:T(8,128)} %get-tuple-element.235, f32[8,256]{1,0:T(8,128)S(1)} %get-tuple-element.236, pred[256,2048]{0,1:T(8,128)(4,1)S(1)} %fusion.35, f32[256,8]{0,1:T(8,128)S(1)} %bitcast.96, bf16[2048,1024]{1,0:T(8,128)(2,1)} %get-tuple-element.265, s32[]{:T(128)S(6)} %select_n.147), kind=kOutput, calls=%fused_computation.17.clone.1 | convolution fusion | flops 1091043328 | bytes 18366468 | tf_op jit(solution)/shard_map/while/body/eval_jaxpr/gqk,kd->qgd/dot_general | solution.py:71
  272.6 0.8 constant_dynamic-update-slice_fusion.2
  274.0 1.1 constant_dynamic-slice_fusion.2
  275.3 8.2 %fusion.36 = (f32[8,256]{1,0:T(8,128)S(1)}, f32[2048,256,8]{1,0,2:T(8,128)}) fusion(pred[256,2048]{0,1:T(8,128)(4,1)S(1)} %fusion.35, bf16[256,8,128]{0,2,1:T(8,128)(2,1)S(1)} %bitcast.85, bf16[2048,1024]{1,0:T(8,128)(2,1)} %get-tuple-element.266, s32[]{:T(128)S(6)} %select_n.147), kind=kOutput, calls=%fused_computation.11.clone.1 | convolution fusion | flops 1086322688 | bytes 18358276 | tf_op jit(solution)/shard_map/while/body/eval_jaxpr/qgd,kd->gqk/dot_general | solution.py:63
  283.5 9.2 %fusion.37 = f32[8,256]{1,0:T(8,128)S(1)} fusion(f32[2048,256,8]{1,0,2:T(8,128)} %get-tuple-element.235, f32[8,256]{1,0:T(8,128)S(1)} %get-tuple-element.236, pred[256,2048]{0,1:T(8,128)(4,1)S(1)} %fusion.35), kind=kLoop, calls=%fused_computation.9.clone.1 | loop fusion | flops 16775168 | bytes 17317888 | tf_op jit(solution)/shard_map/while/body/eval_jaxpr/reduce_sum | solution.py:69
  292.7 10.1 %divide_convert_fusion.2 = bf16[256,8,128]{0,2,1:T(8,128)(2,1)S(1)} fusion(f32[2048,256,8]{1,0,2:T(8,128)} %get-tuple-element.235, f32[8,256]{1,0:T(8,128)S(1)} %get-tuple-element.236, pred[256,2048]{0,1:T(8,128)(4,1)S(1)} %fusion.35, f32[256,8]{0,1:T(8,128)S(1)} %bitcast.96, bf16[2048,1024]{1,0:T(8,128)(2,1)} %get-tuple-element.265, s32[]{:T(128)S(6)} %select_n.147), kind=kOutput, calls=%fused_computation.17.clone.1 | convolution fusion | flops 1091043328 | bytes 18366468 | tf_op jit(solution)/shard_map/while/body/eval_jaxpr/gqk,kd->qgd/dot_general | solution.py:71
  303.0 0.8 constant_dynamic-update-slice_fusion.2
  304.4 1.1 constant_dynamic-slice_fusion.2
  305.6 8.2 %fusion.36 = (f32[8,256]{1,0:T(8,128)S(1)}, f32[2048,256,8]{1,0,2:T(8,128)}) fusion(pred[256,2048]{0,1:T(8,128)(4,1)S(1)} %fusion.35, bf16[256,8,128]{0,2,1:T(8,128)(2,1)S(1)} %bitcast.85, bf16[2048,1024]{1,0:T(8,128)(2,1)} %get-tuple-element.266, s32[]{:T(128)S(6)} %select_n.147), kind=kOutput, calls=%fused_computation.11.clone.1 | convolution fusion | flops 1086322688 | bytes 18358276 | tf_op jit(solution)/shard_map/while/body/eval_jaxpr/qgd,kd->gqk/dot_general | solution.py:63
  313.9 9.2 %fusion.37 = f32[8,256]{1,0:T(8,128)S(1)} fusion(f32[2048,256,8]{1,0,2:T(8,128)} %get-tuple-element.235, f32[8,256]{1,0:T(8,128)S(1)} %get-tuple-element.236, pred[256,2048]{0,1:T(8,128)(4,1)S(1)} %fusion.35), kind=kLoop, calls=%fused_computation.9.clone.1 | loop fusion | flops 16775168 | bytes 17317888 | tf_op jit(solution)/shard_map/while/body/eval_jaxpr/reduce_sum | solution.py:69
  323.0 10.1 %divide_convert_fusion.2 = bf16[256,8,128]{0,2,1:T(8,128)(2,1)S(1)} fusion(f32[2048,256,8]{1,0,2:T(8,128)} %get-tuple-element.235, f32[8,256]{1,0:T(8,128)S(1)} %get-tuple-element.236, pred[256,2048]{0,1:T(8,128)(4,1)S(1)} %fusion.35, f32[256,8]{0,1:T(8,128)S(1)} %bitcast.96, bf16[2048,1024]{1,0:T(8,128)(2,1)} %get-tuple-element.265, s32[]{:T(128)S(6)} %select_n.147), kind=kOutput, calls=%fused_computation.17.clone.1 | convolution fusion | flops 1091043328 | bytes 18366468 | tf_op jit(solution)/shard_map/while/body/eval_jaxpr/gqk,kd->qgd/dot_general | solution.py:71
  333.3 0.8 constant_dynamic-update-slice_fusion.2
  334.2 0.5 fusion.35
  334.7 1.1 constant_dynamic-slice_fusion.2
  336.0 8.2 %fusion.36 = (f32[8,256]{1,0:T(8,128)S(1)}, f32[2048,256,8]{1,0,2:T(8,128)}) fusion(pred[256,2048]{0,1:T(8,128)(4,1)S(1)} %fusion.35, bf16[256,8,128]{0,2,1:T(8,128)(2,1)S(1)} %bitcast.85, bf16[2048,1024]{1,0:T(8,128)(2,1)} %get-tuple-element.266, s32[]{:T(128)S(6)} %select_n.147), kind=kOutput, calls=%fused_computation.11.clone.1 | convolution fusion | flops 1086322688 | bytes 18358276 | tf_op jit(solution)/shard_map/while/body/eval_jaxpr/qgd,kd->gqk/dot_general | solution.py:63
  344.2 9.2 %fusion.37 = f32[8,256]{1,0:T(8,128)S(1)} fusion(f32[2048,256,8]{1,0,2:T(8,128)} %get-tuple-element.235, f32[8,256]{1,0:T(8,128)S(1)} %get-tuple-element.236, pred[256,2048]{0,1:T(8,128)(4,1)S(1)} %fusion.35), kind=kLoop, calls=%fused_computation.9.clone.1 | loop fusion | flops 16775168 | bytes 17317888 | tf_op jit(solution)/shard_map/while/body/eval_jaxpr/reduce_sum | solution.py:69
  353.4 10.1 %divide_convert_fusion.2 = bf16[256,8,128]{0,2,1:T(8,128)(2,1)S(1)} fusion(f32[2048,256,8]{1,0,2:T(8,128)} %get-tuple-element.235, f32[8,256]{1,0:T(8,128)S(1)} %get-tuple-element.236, pred[256,2048]{0,1:T(8,128)(4,1)S(1)} %fusion.35, f32[256,8]{0,1:T(8,128)S(1)} %bitcast.96, bf16[2048,1024]{1,0:T(8,128)(2,1)} %get-tuple-element.265, s32[]{:T(128)S(6)} %select_n.147), kind=kOutput, calls=%fused_computation.17.clone.1 | convolution fusion | flops 1091043328 | bytes 18366468 | tf_op jit(solution)/shard_map/while/body/eval_jaxpr/gqk,kd->qgd/dot_general | solution.py:71
  363.7 0.8 constant_dynamic-update-slice_fusion.2
  365.1 1.1 constant_dynamic-slice_fusion.2
  366.4 8.2 %fusion.36 = (f32[8,256]{1,0:T(8,128)S(1)}, f32[2048,256,8]{1,0,2:T(8,128)}) fusion(pred[256,2048]{0,1:T(8,128)(4,1)S(1)} %fusion.35, bf16[256,8,128]{0,2,1:T(8,128)(2,1)S(1)} %bitcast.85, bf16[2048,1024]{1,0:T(8,128)(2,1)} %get-tuple-element.266, s32[]{:T(128)S(6)} %select_n.147), kind=kOutput, calls=%fused_computation.11.clone.1 | convolution fusion | flops 1086322688 | bytes 18358276 | tf_op jit(solution)/shard_map/while/body/eval_jaxpr/qgd,kd->gqk/dot_general | solution.py:63
  374.6 9.2 %fusion.37 = f32[8,256]{1,0:T(8,128)S(1)} fusion(f32[2048,256,8]{1,0,2:T(8,128)} %get-tuple-element.235, f32[8,256]{1,0:T(8,128)S(1)} %get-tuple-element.236, pred[256,2048]{0,1:T(8,128)(4,1)S(1)} %fusion.35), kind=kLoop, calls=%fused_computation.9.clone.1 | loop fusion | flops 16775168 | bytes 17317888 | tf_op jit(solution)/shard_map/while/body/eval_jaxpr/reduce_sum | solution.py:69
  383.7 10.1 %divide_convert_fusion.2 = bf16[256,8,128]{0,2,1:T(8,128)(2,1)S(1)} fusion(f32[2048,256,8]{1,0,2:T(8,128)} %get-tuple-element.235, f32[8,256]{1,0:T(8,128)S(1)} %get-tuple-element.236, pred[256,2048]{0,1:T(8,128)(4,1)S(1)} %fusion.35, f32[256,8]{0,1:T(8,128)S(1)} %bitcast.96, bf16[2048,1024]{1,0:T(8,128)(2,1)} %get-tuple-element.265, s32[]{:T(128)S(6)} %select_n.147), kind=kOutput, calls=%fused_computation.17.clone.1 | convolution fusion | flops 1091043328 | bytes 18366468 | tf_op jit(solution)/shard_map/while/body/eval_jaxpr/gqk,kd->qgd/dot_general | solution.py:71
  394.1 0.8 constant_dynamic-update-slice_fusion.2
  395.4 1.1 constant_dynamic-slice_fusion.2
  396.7 8.2 %fusion.36 = (f32[8,256]{1,0:T(8,128)S(1)}, f32[2048,256,8]{1,0,2:T(8,128)}) fusion(pred[256,2048]{0,1:T(8,128)(4,1)S(1)} %fusion.35, bf16[256,8,128]{0,2,1:T(8,128)(2,1)S(1)} %bitcast.85, bf16[2048,1024]{1,0:T(8,128)(2,1)} %get-tuple-element.266, s32[]{:T(128)S(6)} %select_n.147), kind=kOutput, calls=%fused_computation.11.clone.1 | convolution fusion | flops 1086322688 | bytes 18358276 | tf_op jit(solution)/shard_map/while/body/eval_jaxpr/qgd,kd->gqk/dot_general | solution.py:63
  404.9 9.2 %fusion.37 = f32[8,256]{1,0:T(8,128)S(1)} fusion(f32[2048,256,8]{1,0,2:T(8,128)} %get-tuple-element.235, f32[8,256]{1,0:T(8,128)S(1)} %get-tuple-element.236, pred[256,2048]{0,1:T(8,128)(4,1)S(1)} %fusion.35), kind=kLoop, calls=%fused_computation.9.clone.1 | loop fusion | flops 16775168 | bytes 17317888 | tf_op jit(solution)/shard_map/while/body/eval_jaxpr/reduce_sum | solution.py:69
  414.1 10.1 %divide_convert_fusion.2 = bf16[256,8,128]{0,2,1:T(8,128)(2,1)S(1)} fusion(f32[2048,256,8]{1,0,2:T(8,128)} %get-tuple-element.235, f32[8,256]{1,0:T(8,128)S(1)} %get-tuple-element.236, pred[256,2048]{0,1:T(8,128)(4,1)S(1)} %fusion.35, f32[256,8]{0,1:T(8,128)S(1)} %bitcast.96, bf16[2048,1024]{1,0:T(8,128)(2,1)} %get-tuple-element.265, s32[]{:T(128)S(6)} %select_n.147), kind=kOutput, calls=%fused_computation.17.clone.1 | convolution fusion | flops 1091043328 | bytes 18366468 | tf_op jit(solution)/shard_map/while/body/eval_jaxpr/gqk,kd->qgd/dot_general | solution.py:71
  424.4 0.8 constant_dynamic-update-slice_fusion.2
  425.8 1.1 constant_dynamic-slice_fusion.2
  427.1 8.2 %fusion.36 = (f32[8,256]{1,0:T(8,128)S(1)}, f32[2048,256,8]{1,0,2:T(8,128)}) fusion(pred[256,2048]{0,1:T(8,128)(4,1)S(1)} %fusion.35, bf16[256,8,128]{0,2,1:T(8,128)(2,1)S(1)} %bitcast.85, bf16[2048,1024]{1,0:T(8,128)(2,1)} %get-tuple-element.266, s32[]{:T(128)S(6)} %select_n.147), kind=kOutput, calls=%fused_computation.11.clone.1 | convolution fusion | flops 1086322688 | bytes 18358276 | tf_op jit(solution)/shard_map/while/body/eval_jaxpr/qgd,kd->gqk/dot_general | solution.py:63
  435.3 9.2 %fusion.37 = f32[8,256]{1,0:T(8,128)S(1)} fusion(f32[2048,256,8]{1,0,2:T(8,128)} %get-tuple-element.235, f32[8,256]{1,0:T(8,128)S(1)} %get-tuple-element.236, pred[256,2048]{0,1:T(8,128)(4,1)S(1)} %fusion.35), kind=kLoop, calls=%fused_computation.9.clone.1 | loop fusion | flops 16775168 | bytes 17317888 | tf_op jit(solution)/shard_map/while/body/eval_jaxpr/reduce_sum | solution.py:69
  444.4 10.1 %divide_convert_fusion.2 = bf16[256,8,128]{0,2,1:T(8,128)(2,1)S(1)} fusion(f32[2048,256,8]{1,0,2:T(8,128)} %get-tuple-element.235, f32[8,256]{1,0:T(8,128)S(1)} %get-tuple-element.236, pred[256,2048]{0,1:T(8,128)(4,1)S(1)} %fusion.35, f32[256,8]{0,1:T(8,128)S(1)} %bitcast.96, bf16[2048,1024]{1,0:T(8,128)(2,1)} %get-tuple-element.265, s32[]{:T(128)S(6)} %select_n.147), kind=kOutput, calls=%fused_computation.17.clone.1 | convolution fusion | flops 1091043328 | bytes 18366468 | tf_op jit(solution)/shard_map/while/body/eval_jaxpr/gqk,kd->qgd/dot_general | solution.py:71
  454.8 0.8 constant_dynamic-update-slice_fusion.2
  455.6 1.0 copy-done.1
  (56 shorter events, 8.1 us)
Async XLA Ops:
  6.5 1.4 copy-start
  6.5 33.4 %copy-start.4 = (s32[1,16]{1,0:T(1,128)S(1)}, s32[1,16]{1,0:T(1,128)}, u32[]{:S(2)}) copy-start(s32[1,16]{1,0:T(1,128)} %param.17) | copy-start | bytes 196
  7.9 50.6 %copy-start.2 = (s32[1,32]{1,0:T(1,128)S(1)}, s32[1,32]{1,0:T(1,128)}, u32[]{:S(2)}) copy-start(s32[1,32]{1,0:T(1,128)} %param.16) | copy-start | bytes 388
  36.2 19.9 %all-to-all-start.1 = ((bf16[16,32,1024]{2,1,0:T(8,128)(2,1)}), bf16[16,32,1024]{2,1,0:T(8,128)(2,1)S(1)}, u32[]{:S(2)}, u32[]{:S(2)}) async-start(bf16[16,32,1024]{2,1,0:T(8,128)(2,1)} %bitcast.89), calls=%async_computation.1 | async-start | bytes 2097152 | tf_op jit(solution)/shard_map/all_to_all | solution.py:33
  39.9 170.4 %all-gather.3.cloned.1.call-start = ((), (), s32[]{:S(2)}) async-start(), calls=%async_computation.3 | async-start | bytes 4718592 | tf_op jit(solution)/shard_map/all_gather | solution.py:39
  73.9 5.7 %copy-start.3 = (s32[1,3]{1,0:T(1,128)S(1)}, s32[1,3]{1,0:T(1,128)}, u32[]{:S(2)}) copy-start(s32[1,3]{1,0:T(1,128)} %param.15) | copy-start | bytes 40
  73.9 125.5 %all-to-all-start.2 = ((bf16[16,32,8192]{2,1,0:T(8,128)(2,1)}), bf16[16,32,8192]{2,1,0:T(8,128)(2,1)}, u32[]{:S(2)}, u32[]{:S(2)}) async-start(bf16[16,32,8192]{2,1,0:T(8,128)(2,1)} %bitcast_select_fusion.1), calls=%async_computation.2 | async-start | bytes 16777216 | tf_op jit(solution)/shard_map/all_to_all | solution.py:32
  78.9 131.4 %all-gather.5.cloned.1.call-start = ((), (), s32[]{:S(2)}) async-start(), calls=%async_computation.4 | async-start | bytes 4718592 | tf_op jit(solution)/shard_map/all_gather | solution.py:38
  455.6 1.0 copy-start.1
Sparse Core Ops, SparseCore 0:
  58.1 28.2 all-gather.2
  88.1 31.9 all-gather.4
where the time goes:
time: 465 us; the launch traced here: 463 us
  matrix products  147 us (32%)
  waiting for transfers between devices  135 us (29%)
  other arithmetic  94 us (20%)
  local copies, waits for them, and re-layouts  40.1 us (9%)
  blocking collectives  24.8 us (5%)
  between operations  13.5 us (3%)
  starting transfers between devices  8.85 us (2%)
    all_to_all x1, waiting for transfers between devices, local(): lax.all_to_all(outgoing(queries), 'cp', split_axis=0, concat_axis=0, tile...  119 us
    dot_general x8, matrix products, single_head_output(): jnp.einsum('gqk,kd->qgd', rounded, value_head, preferred_element_type=jnp...  80.9 us
    reduce_sum x8, other arithmetic, single_head_output(): totals = jnp.sum(weights, axis=2)  73.3 us
    dot_general x8, matrix products, single_head_output(): jnp.einsum('qgd,kd->gqk', query_head, key_head, preferred_element_type=jn...  65.6 us
    all_to_all x1, blocking collectives, local(): lax.all_to_all(outgoing(values), 'cp', split_axis=0, concat_axis=0, tiled...  24.8 us
    all_to_all x1, waiting for transfers between devices, local(): lax.all_to_all(outgoing(keys), 'cp', split_axis=0, concat_axis=0, tiled=T...  15.6 us
    dynamic_slice x16, local copies, waits for them, and re-layouts, single_head_output(): lax.dynamic_slice_in_dim(own_queries, head_number_index * head_width, hea...  10.3 us
    gather x3, local copies, waits for them, and re-layouts, outgoing(): picked = jnp.take(tiled, chosen, axis=0, mode='fill', fill_value=0)  9.52 us
  transfers between devices with their start and end apart: 4, of which 2 were waited for; matrix products, arithmetic and copies ran while one was open for 6% of the time, Pallas kernels for 0%

commit v1 on v0

v1 whole, which is shorter than its diff:
```python
import functools
import math

import jax
import jax.numpy as jnp
from jax import lax
from jax.experimental import pallas as pl
from jax.experimental.pallas import tpu as pltpu
from jax.sharding import PartitionSpec as P

QUERY_HEADS = 64
KEY_VALUE_HEADS = 8
HEAD_SIZE = 128
KEY_BLOCK = 256
MASKED = -1e30


def attention_kernel(bounds, q_ref, k_ref, v_ref, o_ref):
    query_rows = q_ref.shape[0]
    queries_per_group = q_ref.shape[1] // HEAD_SIZE
    score_scale = 1.0 / math.sqrt(HEAD_SIZE)
    first_query = bounds[0]
    lo_block = bounds[1]
    hi_block = bounds[2]
    ends = [bounds[3], bounds[4], bounds[5]]

    def doc_of(pos):
        doc = jnp.zeros(pos.shape, jnp.int32)
        for end in ends:
            doc = doc + (pos >= end).astype(jnp.int32)
        return doc

    query_pos = first_query + lax.broadcasted_iota(jnp.int32, (query_rows, 1), 0)
    query_doc = doc_of(query_pos)

    for head in range(queries_per_group):
        query = q_ref[:, head * HEAD_SIZE:(head + 1) * HEAD_SIZE]

        def body(block, carry):
            row_max, totals, summed = carry
            start = pl.multiple_of(block * KEY_BLOCK, KEY_BLOCK)
            key = k_ref[pl.ds(start, KEY_BLOCK), :]
            value = v_ref[pl.ds(start, KEY_BLOCK), :]
            scores = lax.dot_general(
                query, key, (((1,), (1,)), ((), ())), preferred_element_type=jnp.float32
            ) * score_scale
            key_pos = start + lax.broadcasted_iota(jnp.int32, (1, KEY_BLOCK), 1)
            allowed = (doc_of(key_pos) == query_doc) & (key_pos <= query_pos)
            scores = jnp.where(allowed, scores, MASKED)
            new_max = jnp.maximum(row_max, jnp.max(scores, axis=1, keepdims=True))
            rescale = jnp.exp(row_max - new_max)
            weights = jnp.exp(scores - new_max)
            totals = rescale * totals + jnp.sum(weights, axis=1, keepdims=True)
            summed = rescale * summed + jnp.dot(
                weights.astype(jnp.bfloat16), value, preferred_element_type=jnp.float32
            )
            return new_max, totals, summed

        start_state = (
            jnp.full((query_rows, 1), MASKED, jnp.float32),
            jnp.zeros((query_rows, 1), jnp.float32),
            jnp.zeros((query_rows, HEAD_SIZE), jnp.float32),
        )
        _, totals, summed = lax.fori_loop(lo_block, hi_block, body, start_state)
        o_ref[:, head * HEAD_SIZE:(head + 1) * HEAD_SIZE] = (summed / totals).astype(o_ref.dtype)


def attention(bounds, own_queries, all_keys, all_values, interpret=False):
    tok_rows = own_queries.shape[0]
    group_length = all_keys.shape[0]
    head_width = own_queries.shape[1] // KEY_VALUE_HEADS
    return pl.pallas_call(
        attention_kernel,
        out_shape=jax.ShapeDtypeStruct(own_queries.shape, own_queries.dtype),
        grid_spec=pltpu.PrefetchScalarGridSpec(
            num_scalar_prefetch=1,
            grid=(KEY_VALUE_HEADS,),
            in_specs=[
                pl.BlockSpec((tok_rows, head_width), lambda h, b: (0, h)),
                pl.BlockSpec((group_length, HEAD_SIZE), lambda h, b: (0, h)),
                pl.BlockSpec((group_length, HEAD_SIZE), lambda h, b: (0, h)),
            ],
            out_specs=pl.BlockSpec((tok_rows, head_width), lambda h, b: (0, h)),
        ),
        compiler_params=pltpu.CompilerParams(dimension_semantics=("arbitrary",)),
        interpret=interpret,
    )(bounds, own_queries, all_keys, all_values)


def block_bounds(doc_lengths_row, first_query, tok_rows):
    doc_ends = jnp.cumsum(doc_lengths_row).astype(jnp.int32)
    doc_start = jnp.max(jnp.where(doc_ends <= first_query, doc_ends, 0))
    lo_block = doc_start // KEY_BLOCK
    hi_block = (first_query + tok_rows + KEY_BLOCK - 1) // KEY_BLOCK
    head = jnp.stack([first_query, lo_block, hi_block]).astype(jnp.int32)
    return jnp.concatenate([head, doc_ends, jnp.zeros((2,), jnp.int32)])


def local(queries, keys, values, doc_lengths, send_tile, take_slot):
    tok_rows = queries.shape[0]
    peer_count = lax.axis_size("cp")
    tile_rows = tok_rows // peer_count
    slot_count = send_tile.shape[1] // peer_count
    chosen = send_tile[0]
    placed = take_slot[0]

    def outgoing(source):
        tiled = source.reshape(peer_count, tile_rows, source.shape[1])
        picked = jnp.take(tiled, chosen, axis=0, mode="fill", fill_value=0)
        return picked.reshape(peer_count * slot_count * tile_rows, source.shape[1])

    def incoming(source):
        tiled = source.reshape(peer_count * slot_count, tile_rows, source.shape[1])
        return jnp.take(tiled, placed, axis=0).reshape(tok_rows, source.shape[1])

    got_queries, got_keys, got_values = (
        lax.all_to_all(outgoing(queries), "cp", split_axis=0, concat_axis=0, tiled=True),
        lax.all_to_all(outgoing(keys), "cp", split_axis=0, concat_axis=0, tiled=True),
        lax.all_to_all(outgoing(values), "cp", split_axis=0, concat_axis=0, tiled=True),
    )
    own_queries = incoming(got_queries)
    all_keys, all_values = (
        lax.all_gather(incoming(got_keys), "grp", axis=0, tiled=True),
        lax.all_gather(incoming(got_values), "grp", axis=0, tiled=True),
    )
    member = lax.axis_index("grp")
    bounds = block_bounds(doc_lengths[0], member * tok_rows, tok_rows)
    return attention(bounds, own_queries, all_keys, all_values)


def solution(mesh):
    return jax.shard_map(
        local,
        mesh=mesh,
        in_specs=(
            P(("cp", "grp"), None),
            P(("cp", "grp"), None),
            P(("cp", "grp"), None),
            P("cp", None),
            P(("cp", "grp"), None),
            P(("cp", "grp"), None),
        ),
        out_specs=P(("cp", "grp"), None),
        check_vma=False,
    )
```

time: 465 us -> 421 us (0.905)
  the two profiles are of different devices: /device:TPU:16 before, /device:TPU:90 now
where the time goes in v1:
time: 421 us; the launch traced here: 418 us
  Pallas kernels  205 us (49%)
  waiting for transfers between devices  125 us (30%)
  blocking collectives  21 us (5%)
  local copies, waits for them, and re-layouts  18.4 us (4%)
  other arithmetic  17.9 us (4%)
  between operations  16 us (4%)
  starting transfers between devices  14.8 us (4%)
    pallas_call x1, Pallas kernels, attention(): pl.pallas_call(attention_kernel, out_shape=jax.ShapeDtypeStruct(own_queri...  205 us
    all_to_all x1, waiting for transfers between devices, local(): lax.all_to_all(outgoing(queries), 'cp', split_axis=0, concat_axis=0, tile...  112 us
    all_to_all x1, blocking collectives, local(): lax.all_to_all(outgoing(values), 'cp', split_axis=0, concat_axis=0, tiled...  21 us
    all_to_all x1, waiting for transfers between devices, local(): lax.all_to_all(outgoing(keys), 'cp', split_axis=0, concat_axis=0, tiled=T...  12.2 us
    select_n x4, other arithmetic, outgoing(): picked = jnp.take(tiled, chosen, axis=0, mode='fill', fill_value=0)  9.81 us
    gather x3, local copies, waits for them, and re-layouts, outgoing(): picked = jnp.take(tiled, chosen, axis=0, mode='fill', fill_value=0)  9.4 us
  transfers between devices with their start and end apart: 4, of which 2 were waited for; matrix products, arithmetic and copies ran while one was open for 7% of the time, Pallas kernels for 0%

profile of v1, /device:TPU:90, one launch (start us, length us, event | category | flops | bytes accessed | tf_op | source)
XLA Modules:
  0.0 418.2 jit_solution(6659463025033981430)
XLA Ops:
  6.5 0.0 copy-start
  6.5 0.7 compare_select_fusion.1
  7.3 0.7 compare_and_fusion.1
  7.9 0.0 copy-done
  7.9 0.6 gather_fusion.4
  8.6 1.7 gather_fusion.2
  10.2 0.0 copy-start.3
  10.2 1.2 broadcast_select_fusion
  11.4 0.0 copy-start.1
  11.4 21.0 %all_to_all.24 = bf16[16,32,1024]{2,1,0:T(8,128)(2,1)S(1)} all-to-all(bf16[16,32,1024]{2,1,0:T(8,128)(2,1)S(1)} %bitcast.42), channel_id=1, replica_groups=mesh['cp'=16,'grp'=8] {'cp'}, dimensions={0} | all-to-all | bytes 2097152 | tf_op jit(solution)/shard_map/all_to_all | solution.py:119
  32.4 7.1 %all-to-all-start.1 = ((bf16[16,32,1024]{2,1,0:T(8,128)(2,1)}), bf16[16,32,1024]{2,1,0:T(8,128)(2,1)S(1)}, u32[]{:S(2)}, u32[]{:S(2)}) async-start(bf16[16,32,1024]{2,1,0:T(8,128)(2,1)} %bitcast.41), calls=%async_computation.1 | async-start | bytes 2097152 | tf_op jit(solution)/shard_map/all_to_all | solution.py:118
  39.5 0.0 all-gather.3.cloned.1.call-start
  39.5 0.0 copy-done.3
  39.6 0.6 gather_fusion.5
  40.2 12.2 %all-to-all-done.1 = bf16[16,32,1024]{2,1,0:T(8,128)(2,1)S(1)} async-done(((bf16[16,32,1024]{2,1,0:T(8,128)(2,1)}), bf16[16,32,1024]{2,1,0:T(8,128)(2,1)S(1)}, u32[]{:S(2)}, u32[]{:S(2)}) %all-to-all-start.1) | async-done | bytes 1048608 | tf_op jit(solution)/shard_map/all_to_all | solution.py:118
  52.4 0.6 gather_fusion.3
  53.0 1.2 broadcast_select_fusion.2
  54.2 0.0 all-gather.3.cloned.1.call-update
  54.2 0.5 broadcast.124
  54.7 0.0 copy-done.1
  54.8 0.7 reduce.3
  55.4 0.1 squeeze.14
  55.5 0.1 copy.7
  55.6 0.1 copy.8
  55.7 7.1 %gather_fusion = bf16[32,16,8192]{2,1,0:T(8,128)(2,1)} fusion(bf16[16,16,8192]{2,1,0:T(8,128)(2,1)} %bitcast.40, s32[1024]{0:T(1024)S(1)} %pad_clamp_fusion.3), kind=kCustom, calls=%fused_computation.4 | custom fusion | bytes 16777344 | tf_op jit(solution)/shard_map/jit(_take)/gather | solution.py:109
  62.9 7.9 %bitcast_select_fusion = bf16[16,32,8192]{2,1,0:T(8,128)(2,1)} fusion(pred[16,32]{1,0:T(8,128)(4,1)S(1)} %copy.8, bf16[16,32,8192]{2,1,0:T(8,128)(2,1)} %bitcast.39), kind=kLoop, calls=%fused_computation.6 | loop fusion | flops 4194304 | bytes 16777728 | tf_op jit(solution)/shard_map/jit(_take)/select_n | solution.py:109
  70.8 0.0 copy-start.2
  70.8 7.7 %all-to-all-start = ((bf16[16,32,8192]{2,1,0:T(8,128)(2,1)}), bf16[16,32,8192]{2,1,0:T(8,128)(2,1)}, u32[]{:S(2)}, u32[]{:S(2)}) async-start(bf16[16,32,8192]{2,1,0:T(8,128)(2,1)} %bitcast_select_fusion), calls=%async_computation | async-start | bytes 16777216 | tf_op jit(solution)/shard_map/all_to_all | solution.py:117
  78.4 0.0 all-gather.5.cloned.1.call-start
  78.5 0.7 all-gather.5.cloned.1.call-update
  79.2 0.0 copy-done.2
  79.2 0.2 reduce-window.9
  79.4 0.7 fusion
  82.6 0.1 broadcast_in_dim.51
  82.7 0.1 broadcast_in_dim.52
  82.8 0.7 concatenate.3.bounds
  83.4 111.7 %all-to-all-done = bf16[16,32,8192]{2,1,0:T(8,128)(2,1)} async-done(((bf16[16,32,8192]{2,1,0:T(8,128)(2,1)}), bf16[16,32,8192]{2,1,0:T(8,128)(2,1)}, u32[]{:S(2)}, u32[]{:S(2)}) %all-to-all-start) | async-done | bytes 8388640 | tf_op jit(solution)/shard_map/all_to_all | solution.py:117
  195.1 6.2 %gather_fusion.1 = bf16[16,16,8192]{2,1,0:T(8,128)(2,1)} fusion(bf16[32,16,8192]{2,1,0:T(8,128)(2,1)} %bitcast.11, s32[1024]{0:T(1024)S(1)} %pad_clamp_fusion.2), kind=kCustom, calls=%fused_computation.5 | custom fusion | bytes 8388672 | tf_op jit(solution)/shard_map/jit(_take)/gather | solution.py:114
  201.3 4.6 %bitcast_select_fusion.1.q_ref = bf16[256,8192]{1,0:T(8,128)(2,1)} fusion(bf16[16,16,8192]{2,1,0:T(8,128)(2,1)} %gather_fusion.1, pred[256]{0:T(512)(128)(4,1)S(1)} %broadcast_in_dim.52), kind=kLoop, calls=%fused_computation.7 | loop fusion | flops 2097152 | bytes 8388864 | tf_op jit(solution)/shard_map/jit(_take)/select_n | solution.py:114
  205.9 0.0 all-gather.3.cloned.1.call-done.k_ref
  205.9 0.0 all-gather.5.cloned.1.call-done.v_ref
  205.9 205.4 %shard_map.64 = bf16[256,8192]{1,0:T(8,128)(2,1)} custom-call(s32[8]{0:T(128)} %concatenate.3.bounds, bf16[256,8192]{1,0:T(8,128)(2,1)} %bitcast_select_fusion.1.q_ref, bf16[2048,1024]{1,0:T(8,128)(2,1)} %all-gather.3.cloned.1.call-done.k_ref, bf16[2048,1024]{1,0:T(8,128)(2,1)} %all-gather.5.cloned.1.call-done.v_ref), custom_call_target="tpu_custom_call" | custom-call | tf_op jit(solution)/shard_map/pallas_call | solution.py:72
  (11 shorter events, 0.1 us)
Async XLA Ops:
  6.5 1.4 copy-start
  10.2 29.3 %copy-start.3 = (s32[1,16]{1,0:T(1,128)S(1)}, s32[1,16]{1,0:T(1,128)}, u32[]{:S(2)}) copy-start(s32[1,16]{1,0:T(1,128)} %param.15) | copy-start | bytes 196
  11.4 43.3 %copy-start.1 = (s32[1,32]{1,0:T(1,128)S(1)}, s32[1,32]{1,0:T(1,128)}, u32[]{:S(2)}) copy-start(s32[1,32]{1,0:T(1,128)} %param.14) | copy-start | bytes 388
  32.4 20.0 %all-to-all-start.1 = ((bf16[16,32,1024]{2,1,0:T(8,128)(2,1)}), bf16[16,32,1024]{2,1,0:T(8,128)(2,1)S(1)}, u32[]{:S(2)}, u32[]{:S(2)}) async-start(bf16[16,32,1024]{2,1,0:T(8,128)(2,1)} %bitcast.41), calls=%async_computation.1 | async-start | bytes 2097152 | tf_op jit(solution)/shard_map/all_to_all | solution.py:118
  39.5 166.5 %all-gather.3.cloned.1.call-start = ((), (), s32[]{:S(2)}) async-start(), calls=%async_computation.3 | async-start | bytes 4718592 | tf_op jit(solution)/shard_map/all_gather | solution.py:123
  70.8 8.4 %copy-start.2 = (s32[1,3]{1,0:T(1,128)S(1)}, s32[1,3]{1,0:T(1,128)}, u32[]{:S(2)}) copy-start(s32[1,3]{1,0:T(1,128)} %param.13) | copy-start | bytes 40
  70.8 124.4 %all-to-all-start = ((bf16[16,32,8192]{2,1,0:T(8,128)(2,1)}), bf16[16,32,8192]{2,1,0:T(8,128)(2,1)}, u32[]{:S(2)}, u32[]{:S(2)}) async-start(bf16[16,32,8192]{2,1,0:T(8,128)(2,1)} %bitcast_select_fusion), calls=%async_computation | async-start | bytes 16777216 | tf_op jit(solution)/shard_map/all_to_all | solution.py:117
  78.4 127.5 %all-gather.5.cloned.1.call-start = ((), (), s32[]{:S(2)}) async-start(), calls=%async_computation.4 | async-start | bytes 4718592 | tf_op jit(solution)/shard_map/all_gather | solution.py:124
Sparse Core Ops, SparseCore 0:
  54.4 30.7 all-gather.2
  86.8 31.9 all-gather.4

commit v2 on v1

--- a/solution.py
+++ b/solution.py
@@ -20,23 +20,17 @@
     queries_per_group = q_ref.shape[1] // HEAD_SIZE
     score_scale = 1.0 / math.sqrt(HEAD_SIZE)
     first_query = bounds[0]
-    lo_block = bounds[1]
-    hi_block = bounds[2]
-    ends = [bounds[3], bounds[4], bounds[5]]
-
-    def doc_of(pos):
-        doc = jnp.zeros(pos.shape, jnp.int32)
-        for end in ends:
-            doc = doc + (pos >= end).astype(jnp.int32)
-        return doc
+    ends = [bounds[5], bounds[6], bounds[7]]
 
     query_pos = first_query + lax.broadcasted_iota(jnp.int32, (query_rows, 1), 0)
-    query_doc = doc_of(query_pos)
+    query_start = jnp.zeros((query_rows, 1), jnp.int32)
+    for end in ends:
+        query_start = jnp.maximum(query_start, jnp.where(query_pos >= end, end, 0))
 
     for head in range(queries_per_group):
         query = q_ref[:, head * HEAD_SIZE:(head + 1) * HEAD_SIZE]
 
-        def body(block, carry):
+        def body(block, carry, masked):
             row_max, totals, summed = carry
             start = pl.multiple_of(block * KEY_BLOCK, KEY_BLOCK)
             key = k_ref[pl.ds(start, KEY_BLOCK), :]
@@ -44,9 +38,10 @@
             scores = lax.dot_general(
                 query, key, (((1,), (1,)), ((), ())), preferred_element_type=jnp.float32
             ) * score_scale
-            key_pos = start + lax.broadcasted_iota(jnp.int32, (1, KEY_BLOCK), 1)
-            allowed = (doc_of(key_pos) == query_doc) & (key_pos <= query_pos)
-            scores = jnp.where(allowed, scores, MASKED)
+            if masked:
+                key_pos = start + lax.broadcasted_iota(jnp.int32, (1, KEY_BLOCK), 1)
+                allowed = (key_pos >= query_start) & (key_pos <= query_pos)
+                scores = jnp.where(allowed, scores, MASKED)
             new_max = jnp.maximum(row_max, jnp.max(scores, axis=1, keepdims=True))
             rescale = jnp.exp(row_max - new_max)
             weights = jnp.exp(scores - new_max)
@@ -56,12 +51,15 @@
             )
             return new_max, totals, summed
 
-        start_state = (
+        state = (
             jnp.full((query_rows, 1), MASKED, jnp.float32),
             jnp.zeros((query_rows, 1), jnp.float32),
             jnp.zeros((query_rows, HEAD_SIZE), jnp.float32),
         )
-        _, totals, summed = lax.fori_loop(lo_block, hi_block, body, start_state)
+        masked_body = functools.partial(body, masked=True)
+        state = lax.fori_loop(bounds[1], bounds[2], masked_body, state)
+        state = lax.fori_loop(bounds[2], bounds[3], functools.partial(body, masked=False), state)
+        _, totals, summed = lax.fori_loop(bounds[3], bounds[4], masked_body, state)
         o_ref[:, head * HEAD_SIZE:(head + 1) * HEAD_SIZE] = (summed / totals).astype(o_ref.dtype)
 
 
@@ -89,11 +87,17 @@
 
 def block_bounds(doc_lengths_row, first_query, tok_rows):
     doc_ends = jnp.cumsum(doc_lengths_row).astype(jnp.int32)
-    doc_start = jnp.max(jnp.where(doc_ends <= first_query, doc_ends, 0))
-    lo_block = doc_start // KEY_BLOCK
+
+    def doc_start(pos):
+        return jnp.max(jnp.where(doc_ends <= pos, doc_ends, 0))
+
+    diagonal = first_query // KEY_BLOCK
+    lo_block = doc_start(first_query) // KEY_BLOCK
+    full_block = (doc_start(first_query + tok_rows - 1) + KEY_BLOCK - 1) // KEY_BLOCK
+    full_block = jnp.clip(full_block, lo_block, diagonal)
     hi_block = (first_query + tok_rows + KEY_BLOCK - 1) // KEY_BLOCK
-    head = jnp.stack([first_query, lo_block, hi_block]).astype(jnp.int32)
-    return jnp.concatenate([head, doc_ends, jnp.zeros((2,), jnp.int32)])
+    head = jnp.stack([first_query, lo_block, full_block, diagonal, hi_block]).astype(jnp.int32)
+    return jnp.concatenate([head, doc_ends])
 
 
 def local(queries, keys, values, doc_lengths, send_tile, take_slot):

time: 421 us -> 427 us (1.014)
  the two profiles are of different devices: /device:TPU:90 before, /device:TPU:95 now
where the time goes in v2:
time: 427 us; the launch traced here: 423 us
  Pallas kernels  211 us (49%)
  waiting for transfers between devices  124 us (29%)
  blocking collectives  19.4 us (5%)
  local copies, waits for them, and re-layouts  18.4 us (4%)
  other arithmetic  17.2 us (4%)
  between operations  16.5 us (4%)
  starting transfers between devices  15.6 us (4%)
    pallas_call x1, Pallas kernels, attention(): pl.pallas_call(attention_kernel, out_shape=jax.ShapeDtypeStruct(own_queri...  211 us
    all_to_all x1, waiting for transfers between devices, local(): lax.all_to_all(outgoing(queries), 'cp', split_axis=0, concat_axis=0, tile...  112 us
    all_to_all x1, blocking collectives, local(): lax.all_to_all(outgoing(values), 'cp', split_axis=0, concat_axis=0, tiled...  19.4 us
    all_to_all x1, waiting for transfers between devices, local(): lax.all_to_all(outgoing(keys), 'cp', split_axis=0, concat_axis=0, tiled=T...  11.5 us
    gather x3, local copies, waits for them, and re-layouts, outgoing(): picked = jnp.take(tiled, chosen, axis=0, mode='fill', fill_value=0)  9.36 us
    select_n x4, other arithmetic, outgoing(): picked = jnp.take(tiled, chosen, axis=0, mode='fill', fill_value=0)  9.14 us
  transfers between devices with their start and end apart: 4, of which 2 were waited for; matrix products, arithmetic and copies ran while one was open for 7% of the time, Pallas kernels for 0%

profile of v2, /device:TPU:95, one launch (start us, length us, event | category | flops | bytes accessed | tf_op | source)
XLA Modules:
  0.0 422.9 jit_solution(9402082181146484486)
XLA Ops:
  6.5 0.0 copy-start
  6.5 0.7 compare_select_fusion.1
  7.3 0.7 compare_and_fusion.1
  7.9 0.0 copy-done
  7.9 0.6 gather_fusion.4
  8.6 1.7 gather_fusion.2
  10.2 0.0 copy-start.3
  10.2 1.2 broadcast_select_fusion
  11.4 0.0 copy-start.1
  11.4 19.4 %all_to_all.24 = bf16[16,32,1024]{2,1,0:T(8,128)(2,1)S(1)} all-to-all(bf16[16,32,1024]{2,1,0:T(8,128)(2,1)S(1)} %bitcast.45), channel_id=1, replica_groups=mesh['cp'=16,'grp'=8] {'cp'}, dimensions={0} | all-to-all | bytes 2097152 | tf_op jit(solution)/shard_map/all_to_all | solution.py:123
  30.8 7.0 %all-to-all-start.1 = ((bf16[16,32,1024]{2,1,0:T(8,128)(2,1)}), bf16[16,32,1024]{2,1,0:T(8,128)(2,1)S(1)}, u32[]{:S(2)}, u32[]{:S(2)}) async-start(bf16[16,32,1024]{2,1,0:T(8,128)(2,1)} %bitcast.44), calls=%async_computation.1 | async-start | bytes 2097152 | tf_op jit(solution)/shard_map/all_to_all | solution.py:122
  37.8 0.0 all-gather.3.cloned.1.call-start
  37.8 0.0 copy-done.3
  37.9 0.6 gather_fusion.5
  38.5 11.5 %all-to-all-done.1 = bf16[16,32,1024]{2,1,0:T(8,128)(2,1)S(1)} async-done(((bf16[16,32,1024]{2,1,0:T(8,128)(2,1)}), bf16[16,32,1024]{2,1,0:T(8,128)(2,1)S(1)}, u32[]{:S(2)}, u32[]{:S(2)}) %all-to-all-start.1) | async-done | bytes 1048608 | tf_op jit(solution)/shard_map/all_to_all | solution.py:122
  50.0 0.6 gather_fusion.3
  50.6 1.2 broadcast_select_fusion.2
  51.8 0.0 all-gather.3.cloned.1.call-update
  51.8 0.5 broadcast.122
  52.3 0.0 copy-done.1
  52.3 0.7 reduce.3
  53.0 0.1 squeeze.14
  53.1 0.1 copy.7
  53.2 0.1 copy.8
  53.3 7.1 %gather_fusion = bf16[32,16,8192]{2,1,0:T(8,128)(2,1)} fusion(bf16[16,16,8192]{2,1,0:T(8,128)(2,1)} %bitcast.43, s32[1024]{0:T(1024)S(1)} %pad_clamp_fusion.3), kind=kCustom, calls=%fused_computation.4 | custom fusion | bytes 16777344 | tf_op jit(solution)/shard_map/jit(_take)/gather | solution.py:113
  60.4 7.2 %bitcast_select_fusion = bf16[16,32,8192]{2,1,0:T(8,128)(2,1)} fusion(pred[16,32]{1,0:T(8,128)(4,1)S(1)} %copy.8, bf16[16,32,8192]{2,1,0:T(8,128)(2,1)} %bitcast.42), kind=kLoop, calls=%fused_computation.6 | loop fusion | flops 4194304 | bytes 16777728 | tf_op jit(solution)/shard_map/jit(_take)/select_n | solution.py:113
  67.6 0.0 copy-start.2
  67.6 8.3 %all-to-all-start = ((bf16[16,32,8192]{2,1,0:T(8,128)(2,1)}), bf16[16,32,8192]{2,1,0:T(8,128)(2,1)}, u32[]{:S(2)}, u32[]{:S(2)}) async-start(bf16[16,32,8192]{2,1,0:T(8,128)(2,1)} %bitcast_select_fusion), calls=%async_computation | async-start | bytes 16777216 | tf_op jit(solution)/shard_map/all_to_all | solution.py:121
  75.9 0.2 all-gather.5.cloned.1.call-start
  76.2 0.5 all-gather.5.cloned.1.call-update
  76.7 0.0 copy-done.2
  76.7 0.2 reduce-window.9
  76.9 0.7 fusion.1
  80.6 0.1 broadcast_in_dim.52
  80.7 0.1 broadcast_in_dim.53
  80.7 0.7 concatenate.3.bounds
  81.4 112.4 %all-to-all-done = bf16[16,32,8192]{2,1,0:T(8,128)(2,1)} async-done(((bf16[16,32,8192]{2,1,0:T(8,128)(2,1)}), bf16[16,32,8192]{2,1,0:T(8,128)(2,1)}, u32[]{:S(2)}, u32[]{:S(2)}) %all-to-all-start) | async-done | bytes 8388640 | tf_op jit(solution)/shard_map/all_to_all | solution.py:121
  193.8 6.2 %gather_fusion.1 = bf16[16,16,8192]{2,1,0:T(8,128)(2,1)} fusion(bf16[32,16,8192]{2,1,0:T(8,128)(2,1)} %bitcast.13, s32[1024]{0:T(1024)S(1)} %pad_clamp_fusion.2), kind=kCustom, calls=%fused_computation.5 | custom fusion | bytes 8388672 | tf_op jit(solution)/shard_map/jit(_take)/gather | solution.py:118
  200.1 4.6 %bitcast_select_fusion.1.q_ref = bf16[256,8192]{1,0:T(8,128)(2,1)} fusion(bf16[16,16,8192]{2,1,0:T(8,128)(2,1)} %gather_fusion.1, pred[256]{0:T(512)(128)(4,1)S(1)} %broadcast_in_dim.53), kind=kLoop, calls=%fused_computation.7 | loop fusion | flops 2097152 | bytes 8388864 | tf_op jit(solution)/shard_map/jit(_take)/select_n | solution.py:118
  204.6 0.0 all-gather.3.cloned.1.call-done.k_ref
  204.6 0.0 all-gather.5.cloned.1.call-done.v_ref
  204.6 211.5 %shard_map.64 = bf16[256,8192]{1,0:T(8,128)(2,1)} custom-call(s32[8]{0:T(128)} %concatenate.3.bounds, bf16[256,8192]{1,0:T(8,128)(2,1)} %bitcast_select_fusion.1.q_ref, bf16[2048,1024]{1,0:T(8,128)(2,1)} %all-gather.3.cloned.1.call-done.k_ref, bf16[2048,1024]{1,0:T(8,128)(2,1)} %all-gather.5.cloned.1.call-done.v_ref), custom_call_target="tpu_custom_call" | custom-call | tf_op jit(solution)/shard_map/pallas_call | solution.py:70
  (10 shorter events, 0.1 us)
Async XLA Ops:
  6.5 1.4 copy-start
  10.2 27.6 %copy-start.3 = (s32[1,16]{1,0:T(1,128)S(1)}, s32[1,16]{1,0:T(1,128)}, u32[]{:S(2)}) copy-start(s32[1,16]{1,0:T(1,128)} %param.15) | copy-start | bytes 196
  11.4 40.9 %copy-start.1 = (s32[1,32]{1,0:T(1,128)S(1)}, s32[1,32]{1,0:T(1,128)}, u32[]{:S(2)}) copy-start(s32[1,32]{1,0:T(1,128)} %param.14) | copy-start | bytes 388
  30.8 19.2 %all-to-all-start.1 = ((bf16[16,32,1024]{2,1,0:T(8,128)(2,1)}), bf16[16,32,1024]{2,1,0:T(8,128)(2,1)S(1)}, u32[]{:S(2)}, u32[]{:S(2)}) async-start(bf16[16,32,1024]{2,1,0:T(8,128)(2,1)} %bitcast.44), calls=%async_computation.1 | async-start | bytes 2097152 | tf_op jit(solution)/shard_map/all_to_all | solution.py:122
  37.8 166.9 %all-gather.3.cloned.1.call-start = ((), (), s32[]{:S(2)}) async-start(), calls=%async_computation.3 | async-start | bytes 4718592 | tf_op jit(solution)/shard_map/all_gather | solution.py:127
  67.6 9.1 %copy-start.2 = (s32[1,3]{1,0:T(1,128)S(1)}, s32[1,3]{1,0:T(1,128)}, u32[]{:S(2)}) copy-start(s32[1,3]{1,0:T(1,128)} %param.13) | copy-start | bytes 40
  67.6 126.2 %all-to-all-start = ((bf16[16,32,8192]{2,1,0:T(8,128)(2,1)}), bf16[16,32,8192]{2,1,0:T(8,128)(2,1)}, u32[]{:S(2)}, u32[]{:S(2)}) async-start(bf16[16,32,8192]{2,1,0:T(8,128)(2,1)} %bitcast_select_fusion), calls=%async_computation | async-start | bytes 16777216 | tf_op jit(solution)/shard_map/all_to_all | solution.py:121
  75.9 128.7 %all-gather.5.cloned.1.call-start = ((), (), s32[]{:S(2)}) async-start(), calls=%async_computation.4 | async-start | bytes 4718592 | tf_op jit(solution)/shard_map/all_gather | solution.py:128
Sparse Core Ops, SparseCore 0:
  51.9 33.4 all-gather.2
  87.2 31.9 all-gather.4

commit v3 on v2

--- a/solution.py
+++ b/solution.py
@@ -11,14 +11,15 @@
 QUERY_HEADS = 64
 KEY_VALUE_HEADS = 8
 HEAD_SIZE = 128
-KEY_BLOCK = 256
+KEY_BLOCK = 512
+LANES = 128
 MASKED = -1e30
 
 
-def attention_kernel(bounds, q_ref, k_ref, v_ref, o_ref):
+def attention_kernel(bounds, q_ref, k_ref, v_ref, o_ref, max_ref, total_ref, sum_ref):
     query_rows = q_ref.shape[0]
     queries_per_group = q_ref.shape[1] // HEAD_SIZE
-    score_scale = 1.0 / math.sqrt(HEAD_SIZE)
+    exp2_scale = math.log2(math.e) / math.sqrt(HEAD_SIZE)
     first_query = bounds[0]
     ends = [bounds[5], bounds[6], bounds[7]]
 
@@ -27,46 +28,50 @@
     for end in ends:
         query_start = jnp.maximum(query_start, jnp.where(query_pos >= end, end, 0))
 
-    for head in range(queries_per_group):
-        query = q_ref[:, head * HEAD_SIZE:(head + 1) * HEAD_SIZE]
+    max_ref[...] = jnp.full(max_ref.shape, MASKED, jnp.float32)
+    total_ref[...] = jnp.zeros(total_ref.shape, jnp.float32)
+    sum_ref[...] = jnp.zeros(sum_ref.shape, jnp.float32)
 
-        def body(block, carry, masked):
-            row_max, totals, summed = carry
-            start = pl.multiple_of(block * KEY_BLOCK, KEY_BLOCK)
-            key = k_ref[pl.ds(start, KEY_BLOCK), :]
-            value = v_ref[pl.ds(start, KEY_BLOCK), :]
+    def body(block, carry, masked):
+        start = pl.multiple_of(block * KEY_BLOCK, KEY_BLOCK)
+        key = k_ref[pl.ds(start, KEY_BLOCK), :]
+        value = v_ref[pl.ds(start, KEY_BLOCK), :]
+        if masked:
+            key_pos = start + lax.broadcasted_iota(jnp.int32, (1, KEY_BLOCK), 1)
+            allowed = (key_pos >= query_start) & (key_pos <= query_pos)
+        for head in range(queries_per_group):
+            query = q_ref[:, head * HEAD_SIZE:(head + 1) * HEAD_SIZE]
             scores = lax.dot_general(
                 query, key, (((1,), (1,)), ((), ())), preferred_element_type=jnp.float32
-            ) * score_scale
+            ) * exp2_scale
             if masked:
-                key_pos = start + lax.broadcasted_iota(jnp.int32, (1, KEY_BLOCK), 1)
-                allowed = (key_pos >= query_start) & (key_pos <= query_pos)
                 scores = jnp.where(allowed, scores, MASKED)
+            row_max = max_ref[head]
             new_max = jnp.maximum(row_max, jnp.max(scores, axis=1, keepdims=True))
-            rescale = jnp.exp(row_max - new_max)
-            weights = jnp.exp(scores - new_max)
-            totals = rescale * totals + jnp.sum(weights, axis=1, keepdims=True)
-            summed = rescale * summed + jnp.dot(
+            rescale = jnp.exp2(row_max - new_max)
+            weights = jnp.exp2(scores - jnp.tile(new_max, (1, KEY_BLOCK // LANES)))
+            total_ref[head] = rescale * total_ref[head] + jnp.sum(weights, axis=1, keepdims=True)
+            sum_ref[head] = rescale * sum_ref[head] + jnp.dot(
                 weights.astype(jnp.bfloat16), value, preferred_element_type=jnp.float32
             )
-            return new_max, totals, summed
+            max_ref[head] = new_max
+        return carry
 
-        state = (
-            jnp.full((query_rows, 1), MASKED, jnp.float32),
-            jnp.zeros((query_rows, 1), jnp.float32),
-            jnp.zeros((query_rows, HEAD_SIZE), jnp.float32),
-        )
-        masked_body = functools.partial(body, masked=True)
-        state = lax.fori_loop(bounds[1], bounds[2], masked_body, state)
-        state = lax.fori_loop(bounds[2], bounds[3], functools.partial(body, masked=False), state)
-        _, totals, summed = lax.fori_loop(bounds[3], bounds[4], masked_body, state)
-        o_ref[:, head * HEAD_SIZE:(head + 1) * HEAD_SIZE] = (summed / totals).astype(o_ref.dtype)
+    masked_body = functools.partial(body, masked=True)
+    lax.fori_loop(bounds[1], bounds[2], masked_body, 0)
+    lax.fori_loop(bounds[2], bounds[3], functools.partial(body, masked=False), 0)
+    lax.fori_loop(bounds[3], bounds[4], masked_body, 0)
+    for head in range(queries_per_group):
+        o_ref[:, head * HEAD_SIZE:(head + 1) * HEAD_SIZE] = (
+            sum_ref[head] / total_ref[head]
+        ).astype(o_ref.dtype)
 
 
 def attention(bounds, own_queries, all_keys, all_values, interpret=False):
     tok_rows = own_queries.shape[0]
     group_length = all_keys.shape[0]
     head_width = own_queries.shape[1] // KEY_VALUE_HEADS
+    queries_per_group = head_width // HEAD_SIZE
     return pl.pallas_call(
         attention_kernel,
         out_shape=jax.ShapeDtypeStruct(own_queries.shape, own_queries.dtype),
@@ -79,6 +84,11 @@
                 pl.BlockSpec((group_length, HEAD_SIZE), lambda h, b: (0, h)),
             ],
             out_specs=pl.BlockSpec((tok_rows, head_width), lambda h, b: (0, h)),
+            scratch_shapes=[
+                pltpu.VMEM((queries_per_group, tok_rows, LANES), jnp.float32),
+                pltpu.VMEM((queries_per_group, tok_rows, LANES), jnp.float32),
+                pltpu.VMEM((queries_per_group, tok_rows, HEAD_SIZE), jnp.float32),
+            ],
         ),
         compiler_params=pltpu.CompilerParams(dimension_semantics=("arbitrary",)),
         interpret=interpret,

time: 427 us -> 307 us (0.72)
  the two profiles are of different devices: /device:TPU:95 before, /device:TPU:88 now
where the time goes in v3:
time: 307 us; the launch traced here: 306 us
  waiting for transfers between devices  126 us (41%)
  Pallas kernels  92.4 us (30%)
  blocking collectives  21.9 us (7%)
  local copies, waits for them, and re-layouts  18.5 us (6%)
  other arithmetic  17.7 us (6%)
  between operations  16.5 us (5%)
  starting transfers between devices  13.3 us (4%)
    all_to_all x1, waiting for transfers between devices, local(): lax.all_to_all(outgoing(queries), 'cp', split_axis=0, concat_axis=0, tile...  112 us
    pallas_call x1, Pallas kernels, attention(): pl.pallas_call(attention_kernel, out_shape=jax.ShapeDtypeStruct(own_queri...  92.4 us
    all_to_all x1, blocking collectives, local(): lax.all_to_all(outgoing(values), 'cp', split_axis=0, concat_axis=0, tiled...  21.9 us
    all_to_all x1, waiting for transfers between devices, local(): lax.all_to_all(outgoing(keys), 'cp', split_axis=0, concat_axis=0, tiled=T...  13.1 us
    select_n x4, other arithmetic, outgoing(): picked = jnp.take(tiled, chosen, axis=0, mode='fill', fill_value=0)  9.65 us
    gather x3, local copies, waits for them, and re-layouts, outgoing(): picked = jnp.take(tiled, chosen, axis=0, mode='fill', fill_value=0)  9.48 us
    gather x3, local copies, waits for them, and re-layouts, incoming(): return jnp.take(tiled, placed, axis=0).reshape(tok_rows, source.shape[1])  7.37 us
    all_to_all x1, starting transfers between devices, local(): lax.all_to_all(outgoing(queries), 'cp', split_axis=0, concat_axis=0, tile...  6.83 us
  transfers between devices with their start and end apart: 4, of which 2 were waited for; matrix products, arithmetic and copies ran while one was open for 10% of the time, Pallas kernels for 0%

profile of v3, /device:TPU:88, one launch (start us, length us, event | category | flops | bytes accessed | tf_op | source)
XLA Modules:
  0.0 306.3 jit_solution(13973962093280615029)
XLA Ops:
  6.5 0.0 copy-start
  6.5 0.7 compare_select_fusion.1
  7.3 0.7 compare_and_fusion.1
  7.9 0.0 copy-done
  7.9 0.6 gather_fusion.4
  8.6 1.7 gather_fusion.2
  10.2 0.0 copy-start.3
  10.2 1.2 broadcast_select_fusion
  11.4 0.0 copy-start.1
  11.4 21.9 %all_to_all.24 = bf16[16,32,1024]{2,1,0:T(8,128)(2,1)S(1)} all-to-all(bf16[16,32,1024]{2,1,0:T(8,128)(2,1)S(1)} %bitcast.45), channel_id=1, replica_groups=mesh['cp'=16,'grp'=8] {'cp'}, dimensions={0} | all-to-all | bytes 2097152 | tf_op jit(solution)/shard_map/all_to_all | solution.py:133
  33.3 6.2 %all-to-all-start.1 = ((bf16[16,32,1024]{2,1,0:T(8,128)(2,1)}), bf16[16,32,1024]{2,1,0:T(8,128)(2,1)S(1)}, u32[]{:S(2)}, u32[]{:S(2)}) async-start(bf16[16,32,1024]{2,1,0:T(8,128)(2,1)} %bitcast.44), calls=%async_computation.1 | async-start | bytes 2097152 | tf_op jit(solution)/shard_map/all_to_all | solution.py:132
  39.5 0.0 all-gather.3.cloned.1.call-start
  39.6 0.0 copy-done.3
  39.6 0.6 gather_fusion.5
  40.2 13.1 %all-to-all-done.1 = bf16[16,32,1024]{2,1,0:T(8,128)(2,1)S(1)} async-done(((bf16[16,32,1024]{2,1,0:T(8,128)(2,1)}), bf16[16,32,1024]{2,1,0:T(8,128)(2,1)S(1)}, u32[]{:S(2)}, u32[]{:S(2)}) %all-to-all-start.1) | async-done | bytes 1048608 | tf_op jit(solution)/shard_map/all_to_all | solution.py:132
  53.3 0.6 gather_fusion.3
  53.9 1.2 broadcast_select_fusion.2
  55.1 0.0 all-gather.3.cloned.1.call-update
  55.1 0.5 broadcast.122
  55.7 0.0 copy-done.1
  55.7 0.7 reduce.3
  56.3 0.1 squeeze.14
  56.4 0.1 copy.7
  56.5 0.1 copy.8
  56.6 7.2 %gather_fusion = bf16[32,16,8192]{2,1,0:T(8,128)(2,1)} fusion(bf16[16,16,8192]{2,1,0:T(8,128)(2,1)} %bitcast.43, s32[1024]{0:T(1024)S(1)} %pad_clamp_fusion.3), kind=kCustom, calls=%fused_computation.4 | custom fusion | bytes 16777344 | tf_op jit(solution)/shard_map/jit(_take)/gather | solution.py:123
  63.9 7.7 %bitcast_select_fusion = bf16[16,32,8192]{2,1,0:T(8,128)(2,1)} fusion(pred[16,32]{1,0:T(8,128)(4,1)S(1)} %copy.8, bf16[16,32,8192]{2,1,0:T(8,128)(2,1)} %bitcast.42), kind=kLoop, calls=%fused_computation.6 | loop fusion | flops 4194304 | bytes 16777728 | tf_op jit(solution)/shard_map/jit(_take)/select_n | solution.py:123
  71.6 0.0 copy-start.2
  71.6 6.8 %all-to-all-start = ((bf16[16,32,8192]{2,1,0:T(8,128)(2,1)}), bf16[16,32,8192]{2,1,0:T(8,128)(2,1)}, u32[]{:S(2)}, u32[]{:S(2)}) async-start(bf16[16,32,8192]{2,1,0:T(8,128)(2,1)} %bitcast_select_fusion), calls=%async_computation | async-start | bytes 16777216 | tf_op jit(solution)/shard_map/all_to_all | solution.py:131
  78.4 0.2 all-gather.5.cloned.1.call-start
  78.7 0.5 all-gather.5.cloned.1.call-update
  79.2 0.0 copy-done.2
  79.2 0.2 reduce-window.9
  79.4 0.7 fusion.1
  83.1 0.1 broadcast_in_dim.52
  83.1 0.1 broadcast_in_dim.53
  83.2 0.7 concatenate.3.bounds
  83.9 112.4 %all-to-all-done = bf16[16,32,8192]{2,1,0:T(8,128)(2,1)} async-done(((bf16[16,32,8192]{2,1,0:T(8,128)(2,1)}), bf16[16,32,8192]{2,1,0:T(8,128)(2,1)}, u32[]{:S(2)}, u32[]{:S(2)}) %all-to-all-start) | async-done | bytes 8388640 | tf_op jit(solution)/shard_map/all_to_all | solution.py:131
  196.3 6.2 %gather_fusion.1 = bf16[16,16,8192]{2,1,0:T(8,128)(2,1)} fusion(bf16[32,16,8192]{2,1,0:T(8,128)(2,1)} %bitcast.13, s32[1024]{0:T(1024)S(1)} %pad_clamp_fusion.2), kind=kCustom, calls=%fused_computation.5 | custom fusion | bytes 8388672 | tf_op jit(solution)/shard_map/jit(_take)/gather | solution.py:128
  202.5 4.6 %bitcast_select_fusion.1.q_ref = bf16[256,8192]{1,0:T(8,128)(2,1)} fusion(bf16[16,16,8192]{2,1,0:T(8,128)(2,1)} %gather_fusion.1, pred[256]{0:T(512)(128)(4,1)S(1)} %broadcast_in_dim.53), kind=kLoop, calls=%fused_computation.7 | loop fusion | flops 2097152 | bytes 8388864 | tf_op jit(solution)/shard_map/jit(_take)/select_n | solution.py:128
  207.1 0.0 all-gather.3.cloned.1.call-done.k_ref
  207.1 0.0 all-gather.5.cloned.1.call-done.v_ref
  207.1 92.4 %shard_map.64 = bf16[256,8192]{1,0:T(8,128)(2,1)} custom-call(s32[8]{0:T(128)} %concatenate.3.bounds, bf16[256,8192]{1,0:T(8,128)(2,1)} %bitcast_select_fusion.1.q_ref, bf16[2048,1024]{1,0:T(8,128)(2,1)} %all-gather.3.cloned.1.call-done.k_ref, bf16[2048,1024]{1,0:T(8,128)(2,1)} %all-gather.5.cloned.1.call-done.v_ref), custom_call_target="tpu_custom_call" | custom-call | tf_op jit(solution)/shard_map/pallas_call | solution.py:75
  (10 shorter events, 0.1 us)
Async XLA Ops:
  6.5 1.4 copy-start
  10.2 29.3 %copy-start.3 = (s32[1,16]{1,0:T(1,128)S(1)}, s32[1,16]{1,0:T(1,128)}, u32[]{:S(2)}) copy-start(s32[1,16]{1,0:T(1,128)} %param.15) | copy-start | bytes 196
  11.4 44.3 %copy-start.1 = (s32[1,32]{1,0:T(1,128)S(1)}, s32[1,32]{1,0:T(1,128)}, u32[]{:S(2)}) copy-start(s32[1,32]{1,0:T(1,128)} %param.14) | copy-start | bytes 388
  33.3 20.0 %all-to-all-start.1 = ((bf16[16,32,1024]{2,1,0:T(8,128)(2,1)}), bf16[16,32,1024]{2,1,0:T(8,128)(2,1)S(1)}, u32[]{:S(2)}, u32[]{:S(2)}) async-start(bf16[16,32,1024]{2,1,0:T(8,128)(2,1)} %bitcast.44), calls=%async_computation.1 | async-start | bytes 2097152 | tf_op jit(solution)/shard_map/all_to_all | solution.py:132
  39.5 167.6 %all-gather.3.cloned.1.call-start = ((), (), s32[]{:S(2)}) async-start(), calls=%async_computation.3 | async-start | bytes 4718592 | tf_op jit(solution)/shard_map/all_gather | solution.py:137
  71.6 7.6 %copy-start.2 = (s32[1,3]{1,0:T(1,128)S(1)}, s32[1,3]{1,0:T(1,128)}, u32[]{:S(2)}) copy-start(s32[1,3]{1,0:T(1,128)} %param.13) | copy-start | bytes 40
  71.6 124.7 %all-to-all-start = ((bf16[16,32,8192]{2,1,0:T(8,128)(2,1)}), bf16[16,32,8192]{2,1,0:T(8,128)(2,1)}, u32[]{:S(2)}, u32[]{:S(2)}) async-start(bf16[16,32,8192]{2,1,0:T(8,128)(2,1)} %bitcast_select_fusion), calls=%async_computation | async-start | bytes 16777216 | tf_op jit(solution)/shard_map/all_to_all | solution.py:131
  78.4 128.7 %all-gather.5.cloned.1.call-start = ((), (), s32[]{:S(2)}) async-start(), calls=%async_computation.4 | async-start | bytes 4718592 | tf_op jit(solution)/shard_map/all_gather | solution.py:138
Sparse Core Ops, SparseCore 0:
  55.3 29.8 all-gather.2
  86.8 31.9 all-gather.4
